TPU v7x, 128 devices: a whole 4x4x4 slice. The times are simulated.
128 devices in a mesh: dp: 4 (over z_hi, core), mp: 32 (over x, y, z_lo).
Axes of the slice: x: 4, y: 4, z: 4 (z_hi: 2, z_lo: 2; z = z_hi * 2 + z_lo), core: 2. Of those that a mesh axis runs over, the one named last changes fastest.
Arguments:
- residual_input: bfloat16 [2048, 4608], P(('dp', 'mp')), may hold values from -6 to 6
- before_attention_gain: float32 [4608], replicated, may hold values from 0.25 to 1.75
- after_attention_gain: float32 [4608], replicated, may hold values from 0.25 to 1.75
- before_feedforward_gain: float32 [4608], replicated, may hold values from 0.25 to 1.75
- after_feedforward_gain: float32 [4608], replicated, may hold values from 0.25 to 1.75
- query_weight: bfloat16 [4608, 4096], P(None, 'mp'), may hold values from -0.09375 to 0.09375
- key_value_weight: bfloat16 [4608, 2, 32, 128], P(None, None, 'mp'), as said below
- output_weight: bfloat16 [4096, 4608], P('mp'), may hold values from -0.09375 to 0.09375
- gate_matrix: bfloat16 [4608, 20480], P(None, 'mp'), may hold values from -0.09375 to 0.09375
- up_matrix: bfloat16 [4608, 20480], P(None, 'mp'), may hold values from -0.09375 to 0.09375
- down_matrix: bfloat16 [20480, 4608], P('mp'), may hold values from -0.0390625 to 0.0390625
- key_value_cache: bfloat16 [256, 2, 32, 16, 128], P('dp', None, 'mp'), as said below
- projected_lowrank_left: bfloat16 [64, 4608, 16], P('mp'), may hold values from -0.09375 to 0.09375
- projected_lowrank_right: bfloat16 [64, 16, 3, 32, 128], P(None, None, None, 'mp'), as said below
- result_lowrank_left: bfloat16 [64, 4096, 16], P(None, 'mp'), may hold values from -0.09375 to 0.09375
- result_lowrank_right: bfloat16 [64, 16, 4608], P('mp'), may hold values from -1.5 to 1.5
- token_request: int32 [4, 512], P('dp'), may hold values from 0 to 7, never falling along the last dimension, each value on 1 to 256 neighbouring positions
- lowrank_choice_by_prompt: int32 [4, 8], P('dp'), may hold values from 0 to 63
- adapter_position: int32 [64], replicated, may hold values from 0 to 63, each once
- request_pages: int32 [4, 8, 4], replicated, may hold values from 0 to 255
Outputs:
- hidden_out: bfloat16 [2048, 4608], P(('dp', 'mp'))
- kv_new: bfloat16 [2048, 2, 32, 128], P('dp', None, 'mp')
Inputs may be any that keep to these rules, and one draw needn't show every extreme that they name: `key_value_weight`: query heads h and h2 with h // 2 == h2 // 2 have equal key and value weights: they share one key and value head. `key_value_cache`: query heads that share a key and value head have equal cached keys and values. `projected_lowrank_right`: the key and value parts of query heads that share a key and value head are equal. `token_request`: numbers never fall along a group; every request has at least one token. `adapter_position`: each slot once. `request_pages`: pages may repeat within and across requests.
All inputs are finite; a program needn't handle non-finite values.
Results may differ from a plain program's by a relative error of at most 0.035.
Values may be sent and summed in bfloat16 or wider, within the bound.
No kernel may reach another device: no remote copies, remote signals or barrier semaphores. Data moves between devices by JAX's collectives and lax.ppermute only.
A program may use at most 128 MiB of HBM per device.

v0:
```python
import math
import jax
import jax.numpy as jnp
from jax import lax
from jax.sharding import PartitionSpec as P

HIDDEN_BREADTH = 4608
ASKING_CHANNELS = 32
CHANNEL_LENGTH = 128
NUM_LOW_TERMS = 64
LOW_DIMENSION = 16
SHARD_PROMPTS = 8
PPR = 4
PAGE = 16
EPS = 1e-06
SOFTCAP = 50.0
DP_AXES = ("zh", "c")
MP_AXES = ("x", "y", "zl")
MP_STAGES = (("zl",), ("x", "y"))


def gather_mp(values):
    for stage in MP_STAGES:
        values = lax.all_gather(values, stage, axis=0, tiled=True)
    return values


def scatter_mp(values):
    for stage in reversed(MP_STAGES):
        values = lax.psum_scatter(values, stage, scatter_dimension=0, tiled=True)
    return values


def sum_mp(values):
    for stage in MP_STAGES:
        values = lax.psum(values, stage)
    return values


def rms_scale(values, scaling):
    mean_square = jnp.mean(values * values, axis=-1, keepdims=True)
    return values * lax.rsqrt(mean_square + EPS) * scaling


def apply_rotary(values, token_positions):
    half_dim = values.shape[-1] // 2
    frequency = 10000.0 ** (-2.0 * jnp.arange(half_dim, dtype=jnp.float32) / values.shape[-1])
    angles = token_positions.astype(jnp.float32)[:, None] * frequency[None, :]
    cosine = jnp.cos(angles)[:, None, :]
    sine_part = jnp.sin(angles)[:, None, :]
    first_half = values[..., :half_dim]
    second_half = values[..., half_dim:]
    return jnp.concatenate(
        [
            first_half * cosine - second_half * sine_part,
            second_half * cosine + first_half * sine_part,
        ],
        axis=-1,
    )


def positions_of(segments):
    length = segments.shape[0]
    earlier = jnp.sum((segments[None, :] < segments[:, None]).astype(jnp.int32), axis=1)
    return PPR * PAGE + jnp.arange(length, dtype=jnp.int32) - earlier


def capped(scores):
    return SOFTCAP * jnp.tanh(scores / SOFTCAP)


def attend_local(query_rows, keys_new, fresh_values, keys_pre, values_pre, segments):
    scale_factor = 1.0 / math.sqrt(HIDDEN_BREADTH // ASKING_CHANNELS)
    length = segments.shape[0]
    prefix_owner = jnp.arange(keys_pre.shape[1], dtype=jnp.int32) // (PPR * PAGE)
    mask_pre = (prefix_owner[None, :] == segments[:, None])[None]
    ordinal = jnp.arange(length, dtype=jnp.int32)
    mask_new = ((segments[None, :] == segments[:, None]) & (ordinal[None, :] <= ordinal[:, None]))[
        None
    ]
    scores_pre = (
        jnp.einsum("thd,hjd->htj", query_rows, keys_pre, preferred_element_type=jnp.float32)
        * scale_factor
    )
    scores_new = (
        jnp.einsum("thd,uhd->htu", query_rows, keys_new, preferred_element_type=jnp.float32)
        * scale_factor
    )
    weight_pre = jnp.where(mask_pre, jnp.exp(capped(scores_pre)), 0.0)
    weight_new = jnp.where(mask_new, jnp.exp(capped(scores_new)), 0.0)
    totals = jnp.sum(weight_pre, axis=-1, keepdims=True) + jnp.sum(
        weight_new, axis=-1, keepdims=True
    )
    probs_pre = (weight_pre / totals).astype(jnp.bfloat16)
    probs_new = (weight_new / totals).astype(jnp.bfloat16)
    mixture = jnp.einsum("htj,hjd->thd", probs_pre, values_pre, preferred_element_type=jnp.float32)
    mixture = mixture + jnp.einsum(
        "htu,uhd->thd", probs_new, fresh_values, preferred_element_type=jnp.float32
    )
    return mixture.astype(jnp.bfloat16).reshape(length, -1)


def shards(
    residual_input,
    before_attention_gain,
    after_attention_gain,
    before_feedforward_gain,
    after_feedforward_gain,
    query_weight,
    key_value_weight,
    output_weight,
    gate_matrix,
    up_matrix,
    down_matrix,
    key_value_cache,
    projected_lowrank_left,
    projected_lowrank_right,
    result_lowrank_left,
    result_lowrank_right,
    token_request,
    lowrank_choice_by_prompt,
    adapter_position,
    request_pages,
):
    mp_index = lax.axis_index(MP_AXES)
    dp_index = lax.axis_index(DP_AXES)
    residual = residual_input.astype(jnp.float32)
    normed_rows = rms_scale(residual, before_attention_gain).astype(jnp.bfloat16)
    normalized_rows = gather_mp(normed_rows)
    prompt_ordinal = normalized_rows.shape[0]
    channel_window = query_weight.shape[1] // CHANNEL_LENGTH
    query_rows = jnp.dot(normalized_rows, query_weight, preferred_element_type=jnp.float32).reshape(
        prompt_ordinal, channel_window, CHANNEL_LENGTH
    )
    key_value_rows = jnp.dot(
        normalized_rows,
        key_value_weight.reshape(HIDDEN_BREADTH, 2 * channel_window * CHANNEL_LENGTH),
        preferred_element_type=jnp.float32,
    ).reshape(prompt_ordinal, 2, channel_window, CHANNEL_LENGTH)
    segments = token_request[0]
    request_ids = lowrank_choice_by_prompt[0]
    request_range = jnp.arange(SHARD_PROMPTS, dtype=jnp.int32)
    membership = segments[:, None] == request_range[None, :]
    adapter_range = jnp.arange(NUM_LOW_TERMS, dtype=jnp.int32)
    token_adapter = jnp.sum(jnp.where(membership, request_ids[None, :], 0), axis=1)
    token_adapter_slot = jnp.sum(
        jnp.where(token_adapter[:, None] == adapter_range[None, :], adapter_position[None, :], 0),
        axis=1,
    )
    seat_count = projected_lowrank_left.shape[0]
    local_seats = mp_index * seat_count + jnp.arange(seat_count, dtype=jnp.int32)
    seat_factors = jnp.einsum(
        "td,sdk->tsk", normalized_rows, projected_lowrank_left, preferred_element_type=jnp.float32
    )
    seat_here = token_adapter_slot[:, None] == local_seats[None, :]
    lowrank_source = jnp.sum(jnp.where(seat_here[:, :, None], seat_factors, 0.0), axis=1)
    lowrank_source = sum_mp(lowrank_source.astype(jnp.bfloat16))
    choice_mask_table = membership.astype(jnp.bfloat16)
    broadened_lines = (choice_mask_table[:, :, None] * lowrank_source[:, None, :]).reshape(
        prompt_ordinal, SHARD_PROMPTS * LOW_DIMENSION
    )
    raised_result_lines = projected_lowrank_right[request_ids].reshape(
        SHARD_PROMPTS * LOW_DIMENSION, 3 * channel_window * CHANNEL_LENGTH
    )
    adapter_query_key_value = jnp.dot(
        broadened_lines, raised_result_lines, preferred_element_type=jnp.float32
    ).reshape(prompt_ordinal, 3, channel_window, CHANNEL_LENGTH)
    token_positions = positions_of(segments)
    rotary_queries = apply_rotary(
        query_rows + adapter_query_key_value[:, 0], token_positions
    ).astype(jnp.bfloat16)
    rotary_keys = apply_rotary(
        key_value_rows[:, 0] + adapter_query_key_value[:, 1], token_positions
    ).astype(jnp.bfloat16)
    fresh_values = (key_value_rows[:, 1] + adapter_query_key_value[:, 2]).astype(jnp.bfloat16)
    kv_new = jnp.stack([rotary_keys, fresh_values], axis=1)
    own_pages = lax.dynamic_index_in_dim(request_pages, dp_index, 0, keepdims=False).reshape(
        SHARD_PROMPTS * PPR
    )
    whole_pool = lax.all_gather(key_value_cache, DP_AXES, axis=0, tiled=True)
    chosen = whole_pool[own_pages]
    keys_pre = jnp.transpose(chosen[:, 0], (1, 0, 2, 3)).reshape(
        channel_window, SHARD_PROMPTS * PPR * PAGE, CHANNEL_LENGTH
    )
    values_pre = jnp.transpose(chosen[:, 1], (1, 0, 2, 3)).reshape(
        channel_window, SHARD_PROMPTS * PPR * PAGE, CHANNEL_LENGTH
    )
    attended = attend_local(
        rotary_queries, rotary_keys, fresh_values, keys_pre, values_pre, segments
    )
    request_output_down = result_lowrank_left[request_ids]
    request_output_factors = jnp.einsum(
        "tc,rck->trk", attended, request_output_down, preferred_element_type=jnp.float32
    )
    output_adapter_piece = jnp.sum(
        jnp.where(membership[:, :, None], request_output_factors, 0.0), axis=1
    )
    result_lowrank_source = sum_mp(output_adapter_piece).astype(jnp.bfloat16)
    result_seat_lines = result_lowrank_right.shape[0]
    output_slots = mp_index * result_seat_lines + jnp.arange(result_seat_lines, dtype=jnp.int32)
    resident_here = (token_adapter_slot[:, None] == output_slots[None, :]).astype(jnp.bfloat16)
    broadened_result = (resident_here[:, :, None] * result_lowrank_source[:, None, :]).reshape(
        prompt_ordinal, result_seat_lines * LOW_DIMENSION
    )
    raised_window = result_lowrank_right.reshape(result_seat_lines * LOW_DIMENSION, HIDDEN_BREADTH)
    attn_sum = scatter_mp(
        (
            jnp.dot(attended, output_weight, preferred_element_type=jnp.float32)
            + jnp.dot(broadened_result, raised_window, preferred_element_type=jnp.float32)
        ).astype(jnp.bfloat16)
    ).astype(jnp.float32)
    after_attn = (residual + rms_scale(attn_sum, after_attention_gain)).astype(jnp.bfloat16)
    normed_ffw = rms_scale(after_attn.astype(jnp.float32), before_feedforward_gain).astype(
        jnp.bfloat16
    )
    piece = gather_mp(normed_ffw)
    gated = jnp.dot(piece, gate_matrix, preferred_element_type=jnp.float32)
    upward = jnp.dot(piece, up_matrix, preferred_element_type=jnp.float32)
    hidden = (jax.nn.gelu(gated, approximate=True) * upward).astype(jnp.bfloat16)
    ffw_sum = scatter_mp(
        jnp.dot(hidden, down_matrix, preferred_element_type=jnp.float32).astype(jnp.bfloat16)
    ).astype(jnp.float32)
    hidden_out = (
        after_attn.astype(jnp.float32) + rms_scale(ffw_sum, after_feedforward_gain)
    ).astype(jnp.bfloat16)
    return (hidden_out, kv_new)


def solution(mesh):
    fine_mesh = jax.sharding.Mesh(mesh.devices.reshape(2, 2, 4, 4, 2), DP_AXES + MP_AXES)
    return jax.shard_map(
        shards,
        mesh=fine_mesh,
        in_specs=(
            P(DP_AXES + MP_AXES, None),
            P(),
            P(),
            P(),
            P(),
            P(None, MP_AXES),
            P(None, None, MP_AXES, None),
            P(MP_AXES, None),
            P(None, MP_AXES),
            P(None, MP_AXES),
            P(MP_AXES, None),
            P(DP_AXES, None, MP_AXES, None, None),
            P(MP_AXES, None, None),
            P(None, None, None, MP_AXES, None),
            P(None, MP_AXES, None),
            P(MP_AXES, None, None),
            P(DP_AXES, None),
            P(DP_AXES, None),
            P(),
            P(),
        ),
        out_specs=(P(DP_AXES + MP_AXES, None), P(DP_AXES, None, MP_AXES, None)),
        check_vma=False,
    )
```

profile of v0, /device:TPU:1, one launch (start us, length us, event | category | flops | bytes accessed | tf_op | source)
XLA Modules:
  0.0 553.6 jit_solution(13675936725571163932)
XLA Ops:
  8.0 1.1 fusion.31
  10.1 6.8 %all_gather.16 = bf16[32,4608]{1,0:T(8,128)(2,1)} all-gather(bf16[16,4608]{1,0:T(8,128)(2,1)S(1)} %fusion.33), channel_id=1, replica_groups=mesh['zh'=2,'c'=2,'x'=4,'y'=4,'zl'=2] {'zl'}, dimensions={0}, use_global_device_ids=true | all-gather | bytes 442368 | tf_op jit(solution)/shard_map/all_gather | solution.py:24
  18.4 2.1 gather_fusion.2
  20.5 1.7 gather_fusion.1
  23.1 2.3 copy.60
  25.4 2.5 copy.50
  31.4 8.7 %all-gather.4.cloned.1.call-done = bf16[256,2,1,16,128]{4,3,2,1,0:T(8,128)(2,1)} async-done(((bf16[64,2,1,16,128]{4,3,2,1,0:T(8,128)(2,1)}), bf16[256,2,1,16,128]{4,3,2,1,0:T(8,128)(2,1)}) %all-gather.4.cloned.1.call-update) | async-done | bytes 2097168 | tf_op jit(solution)/shard_map/all_gather | solution.py:180
  40.0 2.9 gather_fusion
  42.9 1.7 fusion.81
  44.6 50.0 %all-gather.6.cloned.1.call-done = bf16[512,4608]{1,0:T(8,128)(2,1)} async-done(((bf16[32,4608]{1,0:T(8,128)(2,1)}), bf16[512,4608]{1,0:T(8,128)(2,1)}) %all-gather.6.cloned.1.call-update) | async-done | bytes 4718608 | tf_op jit(solution)/shard_map/all_gather | solution.py:24
  94.5 3.8 fusion.84
  98.4 6.8 %psum.28 = bf16[512,16]{0,1:T(8,128)(2,1)} all-reduce(bf16[512,16]{0,1:T(8,128)(2,1)S(1)} %select_reduce_fusion.2), channel_id=1, replica_groups=mesh['zh'=2,'c'=2,'x'=4,'y'=4,'zl'=2] {'zl'}, use_global_device_ids=true, to_apply=%region_4.5 | all-reduce | flops 8192 | bytes 32768 | tf_op jit(solution)/shard_map/psum | solution.py:36
  105.2 58.5 %psum.29 = bf16[512,16]{0,1:T(8,128)(2,1)S(1)} all-reduce(bf16[512,16]{0,1:T(8,128)(2,1)} %psum.28), channel_id=1, replica_groups=mesh['zh'=2,'c'=2,'x'=4,'y'=4,'zl'=2] {'x','y'}, use_global_device_ids=true, to_apply=%region_5.6 | all-reduce | flops 8192 | bytes 32768 | tf_op jit(solution)/shard_map/psum | solution.py:36
  164.4 1.3 convolution_bitcast_fusion
  165.8 3.9 fusion.19
  169.8 1.7 fusion.22
  173.9 5.6 %psum.30 = f32[512,16]{0,1:T(8,128)S(1)} all-reduce(f32[512,16]{0,1:T(8,128)S(1)} %select_reduce_fusion), channel_id=1, replica_groups=mesh['zh'=2,'c'=2,'x'=4,'y'=4,'zl'=2] {'zl'}, use_global_device_ids=true, to_apply=%region_10.11 | all-reduce | flops 8192 | bytes 65536 | tf_op jit(solution)/shard_map/psum | solution.py:36
  179.5 55.6 %psum.31 = bf16[512,16]{0,1:T(8,128)(2,1)S(1)} all-reduce(f32[512,16]{0,1:T(8,128)S(1)} %psum.30), channel_id=1, replica_groups=mesh['zh'=2,'c'=2,'x'=4,'y'=4,'zl'=2] {'x','y'}, use_global_device_ids=true, to_apply=%region_11.12 | all-reduce | flops 8192 | bytes 49152 | tf_op jit(solution)/shard_map/psum | solution.py:36
  235.2 1.4 fusion.63
  236.6 3.5 fusion
  240.2 105.5 %reduce-scatter.5.cloned.1.call-done = bf16[32,4608]{1,0:T(8,128)(2,1)} async-done(((bf16[512,4608]{1,0:T(8,128)(2,1)}), bf16[32,4608]{1,0:T(8,128)(2,1)}) %reduce-scatter.5.cloned.1.call-update) | async-done | bytes 294928 | tf_op jit(solution)/shard_map/reduce_scatter | solution.py:30
  345.8 17.8 %reduce-scatter.7.cloned.1.call-done = bf16[16,4608]{1,0:T(8,128)(2,1)} async-done(((bf16[32,4608]{1,0:T(8,128)(2,1)}), bf16[16,4608]{1,0:T(8,128)(2,1)}) %reduce-scatter.7.cloned.1.call-update) | async-done | bytes 147472 | tf_op jit(solution)/shard_map/reduce_scatter | solution.py:30
  363.6 1.1 fusion.27
  364.7 1.2 fusion.35
  365.9 5.3 all_gather.18
  371.5 55.4 %all-gather.8.cloned.1.call-done = bf16[512,4608]{1,0:T(8,128)(2,1)} async-done(((bf16[32,4608]{1,0:T(8,128)(2,1)}), bf16[512,4608]{1,0:T(8,128)(2,1)}) %all-gather.8.cloned.1.call-update) | async-done | bytes 4718608 | tf_op jit(solution)/shard_map/all_gather | solution.py:24
  427.0 7.4 %fusion.85 = f32[512,640]{1,0:T(8,128)S(1)} fusion(bf16[512,4608]{1,0:T(8,128)(2,1)} %all-gather.8.cloned.1.call-done, bf16[4608,640]{1,0:T(8,128)(2,1)} %param.28), kind=kOutput, calls=%fused_computation.141 | convolution fusion | flops 3019898880 | bytes 11927552 | tf_op jit(solution)/shard_map/dot_general | solution.py:217
  434.4 14.3 %convolution_convert_fusion = bf16[512,4608]{1,0:T(8,128)(2,1)} fusion(bf16[640,4608]{1,0:T(8,128)(2,1)} %param.30, bf16[512,4608]{1,0:T(8,128)(2,1)} %all-gather.8.cloned.1.call-done, bf16[4608,640]{1,0:T(8,128)(2,1)} %param.29, f32[512,640]{1,0:T(8,128)S(1)} %fusion.85), kind=kOutput, calls=%fused_computation.5 | convolution fusion | flops 6045433856 | bytes 22544384 | tf_op jit(solution)/shard_map/dot_general | solution.py:221
  448.8 77.2 %reduce-scatter.9.cloned.1.call-done = bf16[32,4608]{1,0:T(8,128)(2,1)} async-done(((bf16[512,4608]{1,0:T(8,128)(2,1)}), bf16[32,4608]{1,0:T(8,128)(2,1)}) %reduce-scatter.9.cloned.1.call-update) | async-done | bytes 294928 | tf_op jit(solution)/shard_map/reduce_scatter | solution.py:30
  526.9 17.1 %reduce-scatter.11.cloned.1.call-done = bf16[16,4608]{1,0:T(8,128)(2,1)} async-done(((bf16[32,4608]{1,0:T(8,128)(2,1)}), bf16[16,4608]{1,0:T(8,128)(2,1)}) %reduce-scatter.11.cloned.1.call-update) | async-done | bytes 147472 | tf_op jit(solution)/shard_map/reduce_scatter | solution.py:30
  544.0 1.1 fusion.29
  545.1 1.7 fusion.38
  (101 shorter events, 12.2 us)
Async XLA Ops:
  7.2 229.4 %copy-start = (bf16[128,4608]{1,0:T(8,128)(2,1)S(1)}, bf16[128,4608]{1,0:T(8,128)(2,1)}, u32[]{:S(2)}) copy-start(bf16[128,4608]{1,0:T(8,128)(2,1)} %param.27) | copy-start | bytes 3538948
  7.2 32.9 %all-gather.4.cloned.1.call-start = ((), (), s32[]{:S(2)}) async-start(), calls=%async_computation.4 | async-start | bytes 2621440 | tf_op jit(solution)/shard_map/all_gather | solution.py:180
  7.9 86.6 %all-gather.6.cloned.1.call-start = ((), (), s32[]{:S(2)}) async-start(), calls=%async_computation.5 | async-start | bytes 5013504 | tf_op jit(solution)/shard_map/all_gather | solution.py:24
  16.8 328.9 %reduce-scatter.5.cloned.1.call-start = ((), (), s32[]{:S(2)}) async-start(), calls=%async_computation.6 | async-start | bytes 5013504 | tf_op jit(solution)/shard_map/reduce_scatter | solution.py:30
  23.1 6.1 %copy-start.9 = (s32[1,512]{1,0:T(1,128)S(1)}, s32[1,512]{1,0:T(1,128)}, u32[]{:S(2)}) copy-start(s32[1,512]{1,0:T(1,128)} %param.36) | copy-start | bytes 6148
  23.1 6.1 %copy-start.19 = (s32[1,8]{1,0:T(1,128)S(1)}, s32[1,8]{1,0:T(1,128)}, u32[]{:S(2)}) copy-start(s32[1,8]{1,0:T(1,128)} %param.37) | copy-start | bytes 100
  23.1 6.2 %copy-start.20 = (s32[64]{0:T(128)S(1)}, s32[64]{0:T(128)}, u32[]{:S(2)}) copy-start(s32[64]{0:T(128)} %param.38) | copy-start | bytes 772
  27.9 137.8 %copy-start.3 = (bf16[256,4608]{1,0:T(8,128)(2,1)S(1)}, bf16[256,4608]{1,0:T(8,128)(2,1)}, u32[]{:S(2)}) copy-start(bf16[256,4608]{1,0:T(8,128)(2,1)} %copy.50) | copy-start | bytes 7077892
  94.5 3.9 copy-start.17
  164.4 5.3 slice-start
  165.7 4.0 slice-start.1
  165.7 4.0 copy-start.5
  169.8 1.8 copy-start.16
  169.8 1.8 copy-start.21
  169.8 2.4 copy-start.8
  169.8 2.4 copy-start.10
  169.8 2.4 copy-start.18
  171.5 1.7 copy-start.7
  172.6 1.1 copy-start.2
  172.6 1.2 copy-start.14
  173.1 62.0 %copy-start.6 = (bf16[2,16,4608]{2,1,0:T(8,128)(2,1)S(1)}, bf16[2,16,4608]{2,1,0:T(8,128)(2,1)}, u32[]{:S(2)}) copy-start(bf16[2,16,4608]{2,1,0:T(8,128)(2,1)} %param.35) | copy-start | bytes 884740
  173.1 62.0 %copy-start.15 = (bf16[512,2]{0,1:T(2,128)(2,1)S(1)}, bf16[512,2]{0,1:T(2,128)(2,1)}, u32[]{:S(2)}) copy-start(bf16[512,2]{0,1:T(2,128)(2,1)} %get-tuple-element.14) | copy-start | bytes 6148
  240.1 124.5 %copy-start.4 = (bf16[16,4608]{1,0:T(8,128)(2,1)S(1)}, bf16[16,4608]{1,0:T(8,128)(2,1)}, u32[]{:S(2)}) copy-start(bf16[16,4608]{1,0:T(8,128)(2,1)} %param.20) | copy-start | bytes 442372
  240.1 124.5 %copy-start.11 = (f32[4608]{0:T(1024)S(1)}, f32[4608]{0:T(1024)}, u32[]{:S(2)}) copy-start(f32[4608]{0:T(1024)} %param.22) | copy-start | bytes 55300
  240.1 125.7 %copy-start.12 = (f32[4608]{0:T(1024)S(1)}, f32[4608]{0:T(1024)}, u32[]{:S(2)}) copy-start(f32[4608]{0:T(1024)} %param.23) | copy-start | bytes 55300
  240.2 123.4 %reduce-scatter.7.cloned.1.call-start = ((), (), s32[]{:S(2)}) async-start(), calls=%async_computation.7 | async-start | bytes 442368 | tf_op jit(solution)/shard_map/reduce_scatter | solution.py:30
  345.7 81.2 %all-gather.8.cloned.1.call-start = ((), (), s32[]{:S(2)}) async-start(), calls=%async_computation.8 | async-start | bytes 5013504 | tf_op jit(solution)/shard_map/all_gather | solution.py:24
  371.3 154.7 %reduce-scatter.9.cloned.1.call-start = ((), (), s32[]{:S(2)}) async-start(), calls=%async_computation.9 | async-start | bytes 5013504 | tf_op jit(solution)/shard_map/reduce_scatter | solution.py:30
  434.4 112.4 %copy-start.1 = (bf16[128,4608]{1,0:T(8,128)(2,1)S(1)}, bf16[128,4608]{1,0:T(8,128)(2,1)}, u32[]{:S(2)}) copy-start(bf16[128,4608]{1,0:T(8,128)(2,1)} %param.27) | copy-start | bytes 3538948
  448.7 96.3 %copy-start.13 = (f32[4608]{0:T(1024)S(1)}, f32[4608]{0:T(1024)}, u32[]{:S(2)}) copy-start(f32[4608]{0:T(1024)} %param.24) | copy-start | bytes 55300
  448.7 95.2 %reduce-scatter.11.cloned.1.call-start = ((), (), s32[]{:S(2)}) async-start(), calls=%async_computation.10 | async-start | bytes 442368 | tf_op jit(solution)/shard_map/reduce_scatter | solution.py:30
Sparse Core Ops, SparseCore 0:
  9.7 30.3 all-gather.3
  42.2 52.2 all-gather.5
  240.3 105.3 reduce-scatter.4
  347.9 15.6 reduce-scatter.6
  371.4 55.4 all-gather.7
  448.9 77.0 reduce-scatter.8
  528.3 15.6 reduce-scatter.10
where the time goes:
time: 554 us
  waiting for transfers between devices  332 us (60%)
  blocking collectives  139 us (25%)
  matrix products  39 us (7%)
  local copies, waits for them, and re-layouts  15.9 us (3%)
  between operations  14.6 us (3%)
  other arithmetic  12.7 us (2%)
    reduce_scatter x4, waiting for transfers between devices, scatter_mp(): values = lax.psum_scatter(values, stage, scatter_dimension=0, tiled=True)  218 us
    psum x4, blocking collectives, sum_mp(): values = lax.psum(values, stage)  127 us
    all_gather x2, waiting for transfers between devices, gather_mp(): values = lax.all_gather(values, stage, axis=0, tiled=True)  105 us
    dot_general x1, matrix products, shards(): jnp.dot(hidden, down_matrix, preferred_element_type=jnp.float32)  14.3 us
    all_gather x2, blocking collectives, gather_mp(): values = lax.all_gather(values, stage, axis=0, tiled=True)  12.1 us
  transfers between devices with their start and end apart: 7, of which 7 were waited for; matrix products, arithmetic and copies ran while one was open for 4% of the time, Pallas kernels for 0%

commit v1 on v0

--- a/solution.py
+++ b/solution.py
@@ -21,7 +21,9 @@
 
 def gather_mp(values):
     for stage in MP_STAGES:
-        values = lax.all_gather(values, stage, axis=0, tiled=True)
+        values = jnp.concatenate(
+            lax.all_to_all(jnp.stack([values] * lax.axis_size(stage)), stage, 0, 0), axis=0
+        )
     return values
 
 

time: 554 us -> 557 us (level)
  waiting for transfers between devices: 332 us -> 260 us
  blocking collectives: 139 us -> 207 us
  starting transfers between devices: 0.46 us -> 7.13 us
    all_gather x2 -> x0, waiting for transfers between devices: 105 us -> none  [gather_mp(): values = lax.all_gather(values, stage, axis=0, tiled=True)]
    all_to_all x0 -> x3, blocking collectives: none -> 76.2 us  [gather_mp(): lax.all_to_all(jnp.stack([values] * lax.axis_size(stage)), stage, 0, 0)]
    all_to_all x0 -> x1, waiting for transfers between devices: none -> 19.8 us  [gather_mp(): lax.all_to_all(jnp.stack([values] * lax.axis_size(stage)), stage, 0, 0)]
    all_gather x2 -> x0, blocking collectives: 12.1 us -> none  [gather_mp(): values = lax.all_gather(values, stage, axis=0, tiled=True)]
    all_gather x1, waiting for transfers between devices: 8.68 us -> 19.9 us  [shards(): whole_pool = lax.all_gather(key_value_cache, DP_AXES, axis=0, tiled=True)]
    all_to_all x0 -> x1, starting transfers between devices: none -> 6.93 us  [gather_mp(): lax.all_to_all(jnp.stack([values] * lax.axis_size(stage)), stage, 0, 0)]
  transfers between devices with their start and end apart: 7 -> 6, of which waited for: 7 -> 6; matrix products, arithmetic and copies ran while one was open for 4% -> 3% of each run, Pallas kernels for 0% -> 0%
where the time goes in v1:
time: 557 us; the launch traced here: 556 us
  waiting for transfers between devices  260 us (47%)
  blocking collectives  207 us (37%)
  matrix products  36.6 us (7%)
  local copies, waits for them, and re-layouts  19.9 us (4%)
  between operations  14.2 us (3%)
  other arithmetic  11.5 us (2%)
  starting transfers between devices  7.13 us (1%)
    reduce_scatter x4, waiting for transfers between devices, scatter_mp(): values = lax.psum_scatter(values, stage, scatter_dimension=0, tiled=True)  220 us
    psum x4, blocking collectives, sum_mp(): values = lax.psum(values, stage)  130 us
    all_to_all x3, blocking collectives, gather_mp(): lax.all_to_all(jnp.stack([values] * lax.axis_size(stage)), stage, 0, 0)  76.2 us
    all_gather x1, waiting for transfers between devices, shards(): whole_pool = lax.all_gather(key_value_cache, DP_AXES, axis=0, tiled=True)  19.9 us
    all_to_all x1, waiting for transfers between devices, gather_mp(): lax.all_to_all(jnp.stack([values] * lax.axis_size(stage)), stage, 0, 0)  19.8 us
    dot_general x1, matrix products, shards(): jnp.dot(hidden, down_matrix, preferred_element_type=jnp.float32)  14.2 us
  transfers between devices with their start and end apart: 6, of which 6 were waited for; matrix products, arithmetic and copies ran while one was open for 3% of the time, Pallas kernels for 0%

profile of v1, /device:TPU:1, one launch (start us, length us, event | category | flops | bytes accessed | tf_op | source)
XLA Modules:
  0.0 556.2 jit_solution(9754967956445928960)
XLA Ops:
  7.2 1.2 fusion.26
  9.4 8.2 %all_to_all.20 = bf16[2,16,4608]{2,1,0:T(8,128)(2,1)S(1)} all-to-all(bf16[2,16,4608]{2,1,0:T(8,128)(2,1)S(1)} %pad_maximum_fusion), channel_id=1, replica_groups=mesh['zh'=2,'c'=2,'x'=4,'y'=4,'zl'=2] {'zl'}, dimensions={0} | all-to-all | bytes 589824 | tf_op jit(solution)/shard_map/all_to_all | solution.py:25
  17.6 2.6 stack.27
  20.2 6.9 %all-to-all-start.1 = ((bf16[16,32,4608]{2,1,0:T(8,128)(2,1)}), bf16[16,32,4608]{2,1,0:T(8,128)(2,1)}, u32[]{:S(2)}, u32[]{:S(2)}) async-start(bf16[16,32,4608]{2,1,0:T(8,128)(2,1)} %stack.27), calls=%async_computation.1 | async-start | bytes 9437184 | tf_op jit(solution)/shard_map/all_to_all | solution.py:25
  28.8 1.2 gather_fusion.2
  30.0 1.7 gather_fusion.1
  32.5 2.0 copy.60
  34.5 2.6 copy.50
  40.5 19.9 %all-gather.2.cloned.1.call-done = bf16[256,2,1,16,128]{4,3,2,1,0:T(8,128)(2,1)} async-done(((bf16[64,2,1,16,128]{4,3,2,1,0:T(8,128)(2,1)}), bf16[256,2,1,16,128]{4,3,2,1,0:T(8,128)(2,1)}) %all-gather.2.cloned.1.call-update) | async-done | bytes 2097168 | tf_op jit(solution)/shard_map/all_gather | solution.py:182
  60.3 2.9 gather_fusion
  63.2 1.7 fusion.78
  64.9 19.8 %all-to-all-done.1 = bf16[16,32,4608]{2,1,0:T(8,128)(2,1)} async-done(((bf16[16,32,4608]{2,1,0:T(8,128)(2,1)}), bf16[16,32,4608]{2,1,0:T(8,128)(2,1)}, u32[]{:S(2)}, u32[]{:S(2)}) %all-to-all-start.1) | async-done | bytes 4718624 | tf_op jit(solution)/shard_map/all_to_all | solution.py:25
  84.7 3.8 fusion.81
  88.5 8.0 %psum.28 = bf16[512,16]{0,1:T(8,128)(2,1)} all-reduce(bf16[512,16]{0,1:T(8,128)(2,1)S(1)} %select_reduce_fusion.2), channel_id=1, replica_groups=mesh['zh'=2,'c'=2,'x'=4,'y'=4,'zl'=2] {'zl'}, use_global_device_ids=true, to_apply=%region_4.5 | all-reduce | flops 8192 | bytes 32768 | tf_op jit(solution)/shard_map/psum | solution.py:38
  96.5 61.3 %psum.29 = bf16[512,16]{0,1:T(8,128)(2,1)S(1)} all-reduce(bf16[512,16]{0,1:T(8,128)(2,1)} %psum.28), channel_id=1, replica_groups=mesh['zh'=2,'c'=2,'x'=4,'y'=4,'zl'=2] {'x','y'}, use_global_device_ids=true, to_apply=%region_5.6 | all-reduce | flops 8192 | bytes 32768 | tf_op jit(solution)/shard_map/psum | solution.py:38
  157.8 3.8 convolution_bitcast_fusion.1
  162.0 4.1 fusion.17
  168.6 5.5 psum.30
  174.1 55.6 %psum.31 = bf16[512,16]{0,1:T(8,128)(2,1)S(1)} all-reduce(f32[512,16]{0,1:T(8,128)S(1)} %psum.30), channel_id=1, replica_groups=mesh['zh'=2,'c'=2,'x'=4,'y'=4,'zl'=2] {'x','y'}, use_global_device_ids=true, to_apply=%region_11.12 | all-reduce | flops 8192 | bytes 49152 | tf_op jit(solution)/shard_map/psum | solution.py:38
  229.7 1.4 fusion.60
  231.2 3.5 fusion
  234.8 107.7 %reduce-scatter.5.cloned.1.call-done = bf16[32,4608]{1,0:T(8,128)(2,1)} async-done(((bf16[512,4608]{1,0:T(8,128)(2,1)}), bf16[32,4608]{1,0:T(8,128)(2,1)}) %reduce-scatter.5.cloned.1.call-update) | async-done | bytes 294928 | tf_op jit(solution)/shard_map/reduce_scatter | solution.py:32
  342.5 17.9 %reduce-scatter.7.cloned.1.call-done = bf16[16,4608]{1,0:T(8,128)(2,1)} async-done(((bf16[32,4608]{1,0:T(8,128)(2,1)}), bf16[16,4608]{1,0:T(8,128)(2,1)}) %reduce-scatter.7.cloned.1.call-update) | async-done | bytes 147472 | tf_op jit(solution)/shard_map/reduce_scatter | solution.py:32
  361.5 1.2 fusion.30
  362.8 7.1 %all_to_all.21 = bf16[2,16,4608]{2,1,0:T(8,128)(2,1)S(1)} all-to-all(bf16[2,16,4608]{2,1,0:T(8,128)(2,1)S(1)} %pad_maximum_fusion.1), channel_id=1, replica_groups=mesh['zh'=2,'c'=2,'x'=4,'y'=4,'zl'=2] {'zl'}, dimensions={0} | all-to-all | bytes 589824 | tf_op jit(solution)/shard_map/all_to_all | solution.py:25
  370.5 60.9 %all_to_all.22 = bf16[16,32,4608]{2,1,0:T(8,128)(2,1)S(1)} all-to-all(bf16[16,32,4608]{2,1,0:T(8,128)(2,1)S(1)} %stack.30), channel_id=1, replica_groups=mesh['zh'=2,'c'=2,'x'=4,'y'=4,'zl'=2] {'x','y'}, dimensions={0} | all-to-all | bytes 9437184 | tf_op jit(solution)/shard_map/all_to_all | solution.py:25
  431.4 2.2 copy-done.2
  433.5 3.8 fusion.82
  437.4 14.2 %convolution_convert_fusion = bf16[512,4608]{1,0:T(8,128)(2,1)} fusion(bf16[640,4608]{1,0:T(8,128)(2,1)} %param.30, bf16[512,4608]{1,0:T(8,128)(2,1)} %bitcast.108, bf16[4608,640]{1,0:T(8,128)(2,1)} %param.29, f32[512,640]{1,0:T(8,128)S(1)} %fusion.82), kind=kOutput, calls=%fused_computation.5 | convolution fusion | flops 6045433856 | bytes 22544384 | tf_op jit(solution)/shard_map/dot_general | solution.py:223
  451.7 77.5 %reduce-scatter.9.cloned.1.call-done = bf16[32,4608]{1,0:T(8,128)(2,1)} async-done(((bf16[512,4608]{1,0:T(8,128)(2,1)}), bf16[32,4608]{1,0:T(8,128)(2,1)}) %reduce-scatter.9.cloned.1.call-update) | async-done | bytes 294928 | tf_op jit(solution)/shard_map/reduce_scatter | solution.py:32
  530.1 16.9 %reduce-scatter.11.cloned.1.call-done = bf16[16,4608]{1,0:T(8,128)(2,1)} async-done(((bf16[32,4608]{1,0:T(8,128)(2,1)}), bf16[16,4608]{1,0:T(8,128)(2,1)}) %reduce-scatter.11.cloned.1.call-update) | async-done | bytes 147472 | tf_op jit(solution)/shard_map/reduce_scatter | solution.py:32
  548.0 1.7 fusion.33
  (110 shorter events, 13.4 us)
Async XLA Ops:
  7.2 224.0 %copy-start = (bf16[128,4608]{1,0:T(8,128)(2,1)S(1)}, bf16[128,4608]{1,0:T(8,128)(2,1)}, u32[]{:S(2)}) copy-start(bf16[128,4608]{1,0:T(8,128)(2,1)} %param.27) | copy-start | bytes 3538948
  20.2 8.6 %copy-start.23 = (s32[1,8]{1,0:T(1,128)S(1)}, s32[1,8]{1,0:T(1,128)}, u32[]{:S(2)}) copy-start(s32[1,8]{1,0:T(1,128)} %param.37) | copy-start | bytes 100
  20.2 8.6 %copy-start.9 = (bf16[64,128,16]{1,2,0:T(8,128)(2,1)S(1)}, bf16[64,128,16]{1,2,0:T(8,128)(2,1)}, u32[]{:S(2)}) copy-start(bf16[64,128,16]{1,2,0:T(8,128)(2,1)} %param.34) | copy-start | bytes 786436
  20.2 64.4 %all-to-all-start.1 = ((bf16[16,32,4608]{2,1,0:T(8,128)(2,1)}), bf16[16,32,4608]{2,1,0:T(8,128)(2,1)}, u32[]{:S(2)}, u32[]{:S(2)}) async-start(bf16[16,32,4608]{2,1,0:T(8,128)(2,1)} %stack.27), calls=%async_computation.1 | async-start | bytes 9437184 | tf_op jit(solution)/shard_map/all_to_all | solution.py:25
  27.2 33.2 %all-gather.2.cloned.1.call-start = ((), (), s32[]{:S(2)}) async-start(), calls=%async_computation.8 | async-start | bytes 2621440 | tf_op jit(solution)/shard_map/all_gather | solution.py:182
  27.9 314.6 %reduce-scatter.5.cloned.1.call-start = ((), (), s32[]{:S(2)}) async-start(), calls=%async_computation.9 | async-start | bytes 5013504 | tf_op jit(solution)/shard_map/reduce_scatter | solution.py:32
  32.5 5.7 %copy-start.13 = (s32[1,512]{1,0:T(1,128)S(1)}, s32[1,512]{1,0:T(1,128)}, u32[]{:S(2)}) copy-start(s32[1,512]{1,0:T(1,128)} %param.36) | copy-start | bytes 6148
  32.5 5.8 %copy-start.24 = (s32[64]{0:T(128)S(1)}, s32[64]{0:T(128)}, u32[]{:S(2)}) copy-start(s32[64]{0:T(128)} %param.38) | copy-start | bytes 772
  37.1 120.7 %copy-start.4 = (bf16[256,4608]{1,0:T(8,128)(2,1)S(1)}, bf16[256,4608]{1,0:T(8,128)(2,1)}, u32[]{:S(2)}) copy-start(bf16[256,4608]{1,0:T(8,128)(2,1)} %copy.50) | copy-start | bytes 7077892
  84.7 3.9 copy-start.21
  157.8 3.9 copy-start.12
  157.8 3.9 copy-start.7
  157.8 4.2 copy-start.6
  162.0 4.2 copy-start.20
  162.0 4.2 copy-start.25
  162.0 4.8 copy-start.11
  162.0 4.8 copy-start.14
  162.0 4.8 copy-start.22
  166.1 1.7 copy-start.10
  167.8 61.9 %copy-start.8 = (bf16[2,16,4608]{2,1,0:T(8,128)(2,1)S(1)}, bf16[2,16,4608]{2,1,0:T(8,128)(2,1)}, u32[]{:S(2)}) copy-start(bf16[2,16,4608]{2,1,0:T(8,128)(2,1)} %param.35) | copy-start | bytes 884740
  167.8 61.9 %copy-start.19 = (bf16[512,2]{0,1:T(2,128)(2,1)S(1)}, bf16[512,2]{0,1:T(2,128)(2,1)}, u32[]{:S(2)}) copy-start(bf16[512,2]{0,1:T(2,128)(2,1)} %get-tuple-element.14) | copy-start | bytes 6148
  234.7 126.8 %copy-start.5 = (bf16[16,4608]{1,0:T(8,128)(2,1)S(1)}, bf16[16,4608]{1,0:T(8,128)(2,1)}, u32[]{:S(2)}) copy-start(bf16[16,4608]{1,0:T(8,128)(2,1)} %param.20) | copy-start | bytes 442372
  234.7 126.8 %copy-start.15 = (f32[4608]{0:T(1024)S(1)}, f32[4608]{0:T(1024)}, u32[]{:S(2)}) copy-start(f32[4608]{0:T(1024)} %param.22) | copy-start | bytes 55300
  234.7 128.0 %copy-start.16 = (f32[4608]{0:T(1024)S(1)}, f32[4608]{0:T(1024)}, u32[]{:S(2)}) copy-start(f32[4608]{0:T(1024)} %param.23) | copy-start | bytes 55300
  234.7 125.7 %reduce-scatter.7.cloned.1.call-start = ((), (), s32[]{:S(2)}) async-start(), calls=%async_computation.10 | async-start | bytes 442368 | tf_op jit(solution)/shard_map/reduce_scatter | solution.py:32
  342.5 186.7 %reduce-scatter.9.cloned.1.call-start = ((), (), s32[]{:S(2)}) async-start(), calls=%async_computation.11 | async-start | bytes 5013504 | tf_op jit(solution)/shard_map/reduce_scatter | solution.py:32
  370.0 63.5 %slice-start = ((s8[5898240]{0:T(1024)(128)(4,1)}), s8[4194304]{0:T(1024)(128)(4,1)S(1)}, s32[]{:S(2)}) async-start(s8[5898240]{0:T(1024)(128)(4,1)} %bitcast.136), calls=%async_computation.13 | async-start | bytes 8388608
  370.4 63.1 %slice-start.1 = ((s8[5898240]{0:T(1024)(128)(4,1)}), s8[1703936]{0:T(1024)(128)(4,1)S(1)}, s32[]{:S(2)}) async-start(s8[5898240]{0:T(1024)(128)(4,1)} %bitcast.136), calls=%async_computation.14 | async-start | bytes 3407872
  431.4 2.2 copy-start.2
  437.3 112.4 %copy-start.1 = (bf16[128,4608]{1,0:T(8,128)(2,1)S(1)}, bf16[128,4608]{1,0:T(8,128)(2,1)}, u32[]{:S(2)}) copy-start(bf16[128,4608]{1,0:T(8,128)(2,1)} %param.27) | copy-start | bytes 3538948
  451.6 96.4 %copy-start.17 = (f32[4608]{0:T(1024)S(1)}, f32[4608]{0:T(1024)}, u32[]{:S(2)}) copy-start(f32[4608]{0:T(1024)} %param.24) | copy-start | bytes 55300
  451.6 95.3 %reduce-scatter.11.cloned.1.call-start = ((), (), s32[]{:S(2)}) async-start(), calls=%async_computation.12 | async-start | bytes 442368 | tf_op jit(solution)/shard_map/reduce_scatter | solution.py:32
  (2 other events, 2.3 us)
Sparse Core Ops, SparseCore 0:
  29.6 30.6 all-gather.1
  234.9 107.5 reduce-scatter.4
  344.8 15.5 reduce-scatter.6
  451.7 77.3 reduce-scatter.8
  531.3 15.5 reduce-scatter.10
